TPU v7x, 512 devices: a whole 4x4x16 slice. The times are simulated.
512 devices in a mesh: row: 16 (over z), col: 32 (over y, x, core).
Axes of the slice: x: 4, y: 4, z: 16, core: 2. Of those that a mesh axis runs over, the one named last changes fastest.
Arguments:
- node_feats: bfloat16 [262144, 512], P(('row', 'col')), may hold values from -8 to 8
- source_feats: bfloat16 [4096, 512], P('col'), may hold values from -6 to 6
- nbr_blocks: int32 [2048, 8], P(('row', 'col')), may hold values from 0 to 31
- nbr_count: int32 [2048], P(('row', 'col')), may hold values from 1 to 8
- adj_tiles: bfloat16 [2048, 8, 128, 128], P(('row', 'col')), may hold values from -0.1875 to 0.1875
- pos_index: int32 [262144], P(('row', 'col')), may hold values from 0 to 511
- noise_block_rows: int32 [16], replicated, may hold values from 0 to 15
- w_self: bfloat16 [512, 512], replicated, may hold values from -0.25 to 0.25
- w_neigh: bfloat16 [512, 512], replicated, may hold values from -0.25 to 0.25
Outputs:
- grad_self: float32 [512, 512], replicated
- neighbour_weight_gradient: float32 [512, 512], replicated
- loss: float32 [], replicated
All inputs are finite; a program needn't handle non-finite values.
Results may differ from a plain program's by a relative error of at most 0.002.
Values may be sent and summed in bfloat16 or wider, within the bound.
No kernel may reach another device: no remote copies, remote signals or barrier semaphores. Data moves between devices by JAX's collectives and lax.ppermute only.
A program may use at most 64 MiB of HBM per device.

v0:
```python
import jax
import jax.numpy as jnp
from jax import lax
from jax.sharding import PartitionSpec as P

BLOCK = 128
NOISE = 128
softness_divisor = 0.2


def xor_pairs(size, mask):
    return [(i, i ^ mask) for i in range(size)]


REDUCE_STEPS = (
    ("col", 1),
    ("col", 2),
    ("col", 4),
    ("col", 8),
    ("col", 16),
    ("row", 1),
    ("row", 2),
    ("row", 4),
    ("row", 8),
)


def tree_allreduce(buf, extra):
    taken = []
    for axis, mask in REDUCE_STEPS:
        size = lax.axis_size(axis)
        if mask >= size:
            continue
        bit = lax.axis_index(axis) // mask % 2
        half = buf.shape[0] // 2
        keep = lax.dynamic_slice_in_dim(buf, bit * half, half, 0)
        send = lax.dynamic_slice_in_dim(buf, (1 - bit) * half, half, 0)
        got, got_extra = lax.ppermute((send, extra), axis, xor_pairs(size, mask))
        buf = keep + got
        extra = extra + got_extra
        taken.append((axis, mask, bit))
    for axis, mask, bit in reversed(taken):
        size = lax.axis_size(axis)
        got = lax.ppermute(buf, axis, xor_pairs(size, mask))
        rows = buf.shape[0]
        out = jnp.zeros((2 * rows,) + buf.shape[1:], buf.dtype)
        out = lax.dynamic_update_slice_in_dim(out, buf, bit * rows, 0)
        out = lax.dynamic_update_slice_in_dim(out, got, (1 - bit) * rows, 0)
        buf = out
    return (buf, extra)


def embed(pre):
    return pre * lax.rsqrt(jnp.sum(pre * pre, axis=-1, keepdims=True) + 1e-06)


def body(
    node_feats,
    source_feats,
    nbr_blocks,
    nbr_count,
    adj_tiles,
    pos_index,
    noise_block_rows,
    w_self,
    w_neigh,
):
    rows = node_feats.shape[0]
    width = node_feats.shape[1]
    slots = adj_tiles.shape[1]
    highest = lax.Precision.HIGHEST
    nodes = rows * lax.axis_size("row") * lax.axis_size("col")
    scale_factor = 1.0 / softness_divisor
    valid = jnp.arange(slots, dtype=jnp.int32)[None, :] < nbr_count[:, None]
    tiles = adj_tiles * valid[:, :, None, None].astype(jnp.bfloat16)
    piece = lax.all_gather(source_feats, "col", axis=0, tiled=True)
    count = piece.shape[0] // BLOCK
    blocks = piece.reshape(count, BLOCK, width)
    indicator_matrix = (
        nbr_blocks[:, :, None] == jnp.arange(count, dtype=jnp.int32)[None, None, :]
    ).astype(jnp.bfloat16)
    selected = jnp.einsum(
        "bkc,cjd->bkjd", indicator_matrix, blocks, preferred_element_type=jnp.float32
    ).astype(jnp.bfloat16)
    summed = jnp.einsum("bkij,bkjd->bid", tiles, selected, preferred_element_type=jnp.float32)
    agg = summed.reshape(rows, width).astype(jnp.bfloat16)
    pre = jnp.dot(node_feats, w_self, preferred_element_type=jnp.float32) + jnp.dot(
        agg, w_neigh, preferred_element_type=jnp.float32
    )
    emb32, pull = jax.vjp(embed, pre)
    zeta_bf = emb32.astype(jnp.bfloat16)
    candidates = lax.all_gather(zeta_bf[:NOISE], "row", axis=0, tiled=True)
    my_row = lax.axis_index("row")
    my_noise = noise_block_rows[my_row]
    noise_emb = lax.dynamic_slice_in_dim(candidates, my_noise * NOISE, NOISE, 0).astype(jnp.float32)
    zeta = zeta_bf.astype(jnp.float32)
    pairing = (pos_index[:, None] == jnp.arange(rows, dtype=jnp.int32)[None, :]).astype(jnp.float32)
    partner = jnp.dot(pairing, zeta, precision=highest)
    s_pos = jnp.sum(zeta * partner, axis=-1) * scale_factor
    s_neg = jnp.dot(zeta, noise_emb.T, precision=highest) * scale_factor
    loss_part = (jnp.sum(jax.nn.softplus(-s_pos)) + jnp.sum(jax.nn.softplus(s_neg)) / NOISE) / nodes
    grad_pos = -jax.nn.sigmoid(-s_pos) / nodes
    grad_neg = jax.nn.sigmoid(s_neg) / (NOISE * nodes)
    anchor = scale_factor * (
        grad_pos[:, None] * partner + jnp.dot(grad_neg, noise_emb, precision=highest)
    )
    partner_grad = jnp.dot(pairing.T, scale_factor * grad_pos[:, None] * zeta, precision=highest)
    dnoise = scale_factor * jnp.dot(grad_neg.T, zeta, precision=highest)
    groups = lax.axis_size("row")
    collected = lax.all_gather(dnoise.astype(jnp.bfloat16), "row", axis=0, tiled=True)
    owned = (noise_block_rows == my_row).astype(jnp.float32)
    returned = jnp.dot(
        owned[None, :],
        collected.astype(jnp.float32).reshape(groups, NOISE * width),
        precision=highest,
    )
    returned = returned.reshape(NOISE, width)
    dzeta = anchor + partner_grad
    dzeta = dzeta.at[:NOISE].add(returned)
    gpre = pull(dzeta)[0].astype(jnp.bfloat16)
    part_self = jnp.dot(node_feats.T, gpre, preferred_element_type=jnp.float32)
    neighbour_partial = jnp.dot(agg.T, gpre, preferred_element_type=jnp.float32)
    stacked = jnp.concatenate([part_self, neighbour_partial], axis=0)
    total, loss_tile = tree_allreduce(stacked, jnp.broadcast_to(loss_part, (8, 128)))
    grad_self = total[:width]
    neighbour_weight_gradient = total[width:]
    return (grad_self, neighbour_weight_gradient, loss_tile[0, 0])


def solution(mesh):
    in_specs = (
        P(("row", "col"), None),
        P("col", None),
        P(("row", "col"), None),
        P(("row", "col")),
        P(("row", "col"), None, None, None),
        P(("row", "col")),
        P(),
        P(),
        P(),
    )
    out_specs = (P(), P(), P())
    return jax.shard_map(body, mesh=mesh, in_specs=in_specs, out_specs=out_specs, check_vma=False)
```

profile of v0, /device:TPU:2, one launch (start us, length us, event | category | flops | bytes accessed | tf_op | source)
XLA Modules:
  0.0 480.4 jit_solution(14031274713754208656)
XLA Ops:
  8.7 1.5 fusion.43
  10.2 66.5 %all-gather.4.cloned.1.call-done = bf16[4096,512]{1,0:T(8,128)(2,1)} async-done(((bf16[128,512]{1,0:T(8,128)(2,1)}), bf16[4096,512]{1,0:T(8,128)(2,1)}) %all-gather.4.cloned.1.call-update) | async-done | bytes 4194320 | tf_op jit(solution)/shard_map/all_gather | solution.py:76
  76.7 5.5 %fusion.1 = bf16[4,8,128,512]{3,1,2,0:T(8,128)(2,1)S(1)} fusion(bf16[32,128,512,1]{2,1,0,3:T(8,128)(2,1)} %bitcast.40, s32[4,8]{1,0:T(4,128)S(1)} %copy-done.5), kind=kOutput, calls=%fused_computation.2 | convolution fusion | flops 134218752 | bytes 8388736 | tf_op jit(solution)/shard_map/bkc,cjd->bkjd/dot_general | solution.py:82
  82.3 2.6 fusion.8
  87.9 77.2 %all-gather.6.cloned.1.call-done = bf16[2048,512]{0,1:T(8,128)(2,1)} async-done(((bf16[128,512]{0,1:T(8,128)(2,1)}), bf16[2048,512]{0,1:T(8,128)(2,1)}) %all-gather.6.cloned.1.call-update) | async-done | bytes 2097168 | tf_op jit(solution)/shard_map/all_gather | solution.py:92
  165.0 1.9 fusion.21
  169.6 1.6 fusion.7
  172.4 65.5 %all-gather.8.cloned.1.call-done = bf16[2048,512]{1,0:T(8,128)(2,1)} async-done(((bf16[128,512]{1,0:T(8,128)(2,1)}), bf16[2048,512]{1,0:T(8,128)(2,1)}) %all-gather.8.cloned.1.call-update) | async-done | bytes 2097168 | tf_op jit(solution)/shard_map/all_gather | solution.py:110
  238.0 3.1 reshape.99
  241.1 2.0 fusion.3
  246.8 1.9 collective-permute-start
  248.8 2.9 collective-permute-done
  251.7 1.7 fusion.14
  254.4 2.5 collective-permute-start.1
  256.9 13.3 %collective-permute-done.1 = f32[256,512]{1,0:T(8,128)S(1)} collective-permute-done((f32[256,512]{1,0:T(8,128)S(1)}, f32[256,512]{1,0:T(8,128)S(1)}, u32[]{:S(2)}, u32[]{:S(2)}) %collective-permute-start.1) | collective-permute-done | bytes 524320 | tf_op jit(solution)/shard_map/ppermute | solution.py:38
  271.4 4.0 collective-permute-start.2
  275.4 6.9 %collective-permute-done.2 = f32[128,512]{1,0:T(8,128)S(1)} collective-permute-done((f32[128,512]{1,0:T(8,128)S(1)}, f32[128,512]{1,0:T(8,128)S(1)}, u32[]{:S(2)}, u32[]{:S(2)}) %collective-permute-start.2) | collective-permute-done | bytes 262176 | tf_op jit(solution)/shard_map/ppermute | solution.py:38
  282.4 3.4 collective-permute-start.3
  285.8 3.4 collective-permute-done.3
  289.3 4.9 %collective-permute-start.4 = (f32[32,512]{1,0:T(8,128)S(1)}, f32[32,512]{1,0:T(8,128)S(1)}, u32[]{:S(2)}, u32[]{:S(2)}) collective-permute-start(f32[32,512]{1,0:T(8,128)S(1)} %constant_dynamic-slice_fusion.6), channel_id=1, source_target_pairs={{0,16},{1,17},{2,18},{3,19},{4,20},{5,21},{6,22},{7,23},{8,24},{9,... | collective-permute-start | bytes 196616 | tf_op jit(solution)/shard_map/ppermute | solution.py:38
  294.2 2.7 collective-permute-done.4
  297.0 3.6 collective-permute-start.5
  300.6 2.2 collective-permute-done.5
  302.8 3.4 collective-permute-start.6
  306.2 3.1 collective-permute-done.6
  309.3 5.1 %collective-permute-start.7 = (f32[4,512]{1,0:T(4,128)S(1)}, f32[4,512]{1,0:T(4,128)S(1)}, u32[]{:S(2)}, u32[]{:S(2)}) collective-permute-start(f32[4,512]{1,0:T(4,128)S(1)} %constant_dynamic-slice_fusion.2), channel_id=1, source_target_pairs={{0,128},{32,160},{64,192},{96,224},{128,0},{160,32},{192,64},{224,... | collective-permute-start | bytes 24584 | tf_op jit(solution)/shard_map/ppermute | solution.py:38
  314.5 4.3 collective-permute-done.7
  318.8 8.6 %collective-permute-start.8 = (f32[2,512]{1,0:T(2,128)S(1)}, f32[2,512]{1,0:T(2,128)S(1)}, u32[]{:S(2)}, u32[]{:S(2)}) collective-permute-start(f32[2,512]{1,0:T(2,128)S(1)} %constant_dynamic-slice_fusion), channel_id=1, source_target_pairs={{0,256},{32,288},{64,320},{96,352},{128,384},{160,416},{192,448},{... | collective-permute-start | bytes 12296 | tf_op jit(solution)/shard_map/ppermute | solution.py:38
  327.4 5.6 %collective-permute-done.8 = f32[2,512]{1,0:T(2,128)S(1)} collective-permute-done((f32[2,512]{1,0:T(2,128)S(1)}, f32[2,512]{1,0:T(2,128)S(1)}, u32[]{:S(2)}, u32[]{:S(2)}) %collective-permute-start.8) | collective-permute-done | bytes 4128 | tf_op jit(solution)/shard_map/ppermute | solution.py:38
  333.0 8.6 %collective-permute-start.9 = (f32[2,512]{1,0:T(2,128)S(1)}, f32[2,512]{1,0:T(2,128)S(1)}, u32[]{:S(2)}, u32[]{:S(2)}) collective-permute-start(f32[2,512]{1,0:T(2,128)S(1)} %get-tuple-element.16), channel_id=1, source_target_pairs={{0,256},{32,288},{64,320},{96,352},{128,384},{160,416},{192,448},{... | collective-permute-start | bytes 12296 | tf_op jit(solution)/shard_map/ppermute | solution.py:44
  341.7 5.6 %collective-permute-done.9 = f32[2,512]{1,0:T(2,128)S(1)} collective-permute-done((f32[2,512]{1,0:T(2,128)S(1)}, f32[2,512]{1,0:T(2,128)S(1)}, u32[]{:S(2)}, u32[]{:S(2)}) %collective-permute-start.9) | collective-permute-done | bytes 4128 | tf_op jit(solution)/shard_map/ppermute | solution.py:44
  347.3 5.1 %collective-permute-start.10 = (f32[4,512]{1,0:T(4,128)S(1)}, f32[4,512]{1,0:T(4,128)S(1)}, u32[]{:S(2)}, u32[]{:S(2)}) collective-permute-start(f32[4,512]{1,0:T(4,128)S(1)} %constant_dynamic-update-slice_fusion.16), channel_id=1, source_target_pairs={{0,128},{32,160},{64,192},{96,224},{128,0},{160,32},{192,64},{224,... | collective-permute-start | bytes 24584 | tf_op jit(solution)/shard_map/ppermute | solution.py:44
  352.4 4.3 collective-permute-done.10
  356.7 3.4 collective-permute-start.11
  360.1 3.1 collective-permute-done.11
  363.2 3.6 collective-permute-start.12
  366.8 2.2 collective-permute-done.12
  369.0 4.9 %collective-permute-start.13 = (f32[32,512]{1,0:T(8,128)S(1)}, f32[32,512]{1,0:T(8,128)S(1)}, u32[]{:S(2)}, u32[]{:S(2)}) collective-permute-start(f32[32,512]{1,0:T(8,128)S(1)} %constant_dynamic-update-slice_fusion.10), channel_id=1, source_target_pairs={{0,16},{1,17},{2,18},{3,19},{4,20},{5,21},{6,22},{7,23},{8,24},{9,... | collective-permute-start | bytes 196616 | tf_op jit(solution)/shard_map/ppermute | solution.py:44
  374.0 2.7 collective-permute-done.13
  376.7 3.4 collective-permute-start.14
  380.1 3.4 collective-permute-done.14
  383.6 4.0 collective-permute-start.15
  387.6 5.7 %collective-permute-done.15 = f32[128,512]{1,0:T(8,128)S(1)} collective-permute-done((f32[128,512]{1,0:T(8,128)S(1)}, f32[128,512]{1,0:T(8,128)S(1)}, u32[]{:S(2)}, u32[]{:S(2)}) %collective-permute-start.15) | collective-permute-done | bytes 262176 | tf_op jit(solution)/shard_map/ppermute | solution.py:44
  393.4 2.5 collective-permute-start.16
  396.0 8.4 %collective-permute-done.16 = f32[256,512]{1,0:T(8,128)S(1)} collective-permute-done((f32[256,512]{1,0:T(8,128)S(1)}, f32[256,512]{1,0:T(8,128)S(1)}, u32[]{:S(2)}, u32[]{:S(2)}) %collective-permute-start.16) | collective-permute-done | bytes 524320 | tf_op jit(solution)/shard_map/ppermute | solution.py:44
  404.5 1.9 collective-permute-start.17
  407.7 2.4 collective-permute-start.18
  410.9 2.5 collective-permute-start.19
  413.4 3.0 collective-permute-done.19
  416.4 4.0 collective-permute-start.20
  420.4 3.0 collective-permute-done.20
  423.4 3.4 collective-permute-start.21
  426.8 2.1 collective-permute-done.21
  428.9 4.9 %collective-permute-start.22 = (f32[8,128]{1,0:T(8,128)S(1)}, f32[8,128]{1,0:T(8,128)S(1)}, u32[]{:S(2)}, u32[]{:S(2)}) collective-permute-start(f32[8,128]{1,0:T(8,128)S(1)} %add.274), channel_id=1, source_target_pairs={{0,16},{1,17},{2,18},{3,19},{4,20},{5,21},{6,22},{7,23},{8,24},{9,... | collective-permute-start | bytes 12296 | tf_op jit(solution)/shard_map/ppermute | solution.py:38
  433.8 2.1 collective-permute-done.22
  435.9 3.6 collective-permute-start.23
  439.5 1.9 collective-permute-done.23
  441.4 3.4 collective-permute-start.24
  444.8 3.0 collective-permute-done.24
  447.8 5.1 %collective-permute-start.25 = (f32[8,128]{1,0:T(8,128)S(1)}, f32[8,128]{1,0:T(8,128)S(1)}, u32[]{:S(2)}, u32[]{:S(2)}) collective-permute-start(f32[8,128]{1,0:T(8,128)S(1)} %add.277), channel_id=1, source_target_pairs={{0,128},{32,160},{64,192},{96,224},{128,0},{160,32},{192,64},{224,... | collective-permute-start | bytes 12296 | tf_op jit(solution)/shard_map/ppermute | solution.py:38
  452.9 4.3 collective-permute-done.25
  457.2 8.7 %collective-permute-start.26 = (f32[8,128]{1,0:T(8,128)S(1)}, f32[8,128]{1,0:T(8,128)S(1)}, u32[]{:S(2)}, u32[]{:S(2)}) collective-permute-start(f32[8,128]{1,0:T(8,128)S(1)} %add.278), channel_id=1, source_target_pairs={{0,256},{32,288},{64,320},{96,352},{128,384},{160,416},{192,448},{... | collective-permute-start | bytes 12296 | tf_op jit(solution)/shard_map/ppermute | solution.py:38
  465.9 5.5 %collective-permute-done.26 = f32[8,128]{1,0:T(8,128)S(1)} collective-permute-done((f32[8,128]{1,0:T(8,128)S(1)}, f32[8,128]{1,0:T(8,128)S(1)}, u32[]{:S(2)}, u32[]{:S(2)}) %collective-permute-start.26) | collective-permute-done | bytes 4128 | tf_op jit(solution)/shard_map/ppermute | solution.py:38
  472.4 1.5 fusion.42
  (97 shorter events, 15.7 us)
Async XLA Ops:
  7.2 1.5 copy-start
  7.2 69.5 %copy-start.5 = (s32[4,8]{1,0:T(4,128)S(1)}, s32[4,8]{1,0:T(4,128)}, u32[]{:S(2)}) copy-start(s32[4,8]{1,0:T(4,128)} %param.13) | copy-start | bytes 388
  7.2 69.5 %all-gather.4.cloned.1.call-start = ((), (), s32[]{:S(2)}) async-start(), calls=%async_computation | async-start | bytes 4325376 | tf_op jit(solution)/shard_map/all_gather | solution.py:76
  7.9 157.1 %all-gather.6.cloned.1.call-start = ((), (), s32[]{:S(2)}) async-start(), calls=%async_computation.1 | async-start | bytes 2228224 | tf_op jit(solution)/shard_map/all_gather | solution.py:92
  76.7 5.5 %copy-start.8 = (bf16[4,8,128,128]{3,2,1,0:T(8,128)(2,1)S(1)}, bf16[4,8,128,128]{3,2,1,0:T(8,128)(2,1)}, u32[]{:S(2)}) copy-start(bf16[4,8,128,128]{3,2,1,0:T(8,128)(2,1)} %param.15) | copy-start | bytes 3145732
  82.3 2.6 copy-start.4
  84.9 0.8 copy-start.2
  84.9 1.7 copy-start.7
  85.7 82.7 %copy-start.6 = (s32[512]{0:T(512)S(1)}, s32[512]{0:T(512)}, u32[]{:S(2)}) copy-start(s32[512]{0:T(512)} %param.16) | copy-start | bytes 6148
  86.4 151.6 %all-gather.8.cloned.1.call-start = ((), (), s32[]{:S(2)}) async-start(), calls=%async_computation.2 | async-start | bytes 2228224 | tf_op jit(solution)/shard_map/all_gather | solution.py:110
  243.4 1.0 copy-start.3
  246.8 4.9 %collective-permute-start = (f32[512,512]{1,0:T(8,128)}, f32[512,512]{1,0:T(8,128)}, u32[]{:S(2)}, u32[]{:S(2)}) collective-permute-start(f32[512,512]{1,0:T(8,128)} %fusion.12), channel_id=1, source_target_pairs={{0,1},{1,0},{2,3},{3,2},{4,5},{5,4},{6,7},{7,6},{8,9},{9,8},{10,11... | collective-permute-start | bytes 3145736 | tf_op jit(solution)/shard_map/ppermute | solution.py:38
  253.3 1.0 copy-start.1
  254.4 15.9 %collective-permute-start.1 = (f32[256,512]{1,0:T(8,128)S(1)}, f32[256,512]{1,0:T(8,128)S(1)}, u32[]{:S(2)}, u32[]{:S(2)}) collective-permute-start(f32[256,512]{1,0:T(8,128)S(1)} %constant_dynamic-slice_fusion.9), channel_id=1, source_target_pairs={{0,2},{1,3},{2,0},{3,1},{4,6},{5,7},{6,4},{7,5},{8,10},{9,11},{10,... | collective-permute-start | bytes 1572872 | tf_op jit(solution)/shard_map/ppermute | solution.py:38
  271.4 10.9 %collective-permute-start.2 = (f32[128,512]{1,0:T(8,128)S(1)}, f32[128,512]{1,0:T(8,128)S(1)}, u32[]{:S(2)}, u32[]{:S(2)}) collective-permute-start(f32[128,512]{1,0:T(8,128)S(1)} %constant_dynamic-slice_fusion.8), channel_id=1, source_target_pairs={{0,4},{1,5},{2,6},{3,7},{4,0},{5,1},{6,2},{7,3},{8,12},{9,13},{10,... | collective-permute-start | bytes 786440 | tf_op jit(solution)/shard_map/ppermute | solution.py:38
  282.4 6.9 %collective-permute-start.3 = (f32[64,512]{1,0:T(8,128)S(1)}, f32[64,512]{1,0:T(8,128)S(1)}, u32[]{:S(2)}, u32[]{:S(2)}) collective-permute-start(f32[64,512]{1,0:T(8,128)S(1)} %constant_dynamic-slice_fusion.7), channel_id=1, source_target_pairs={{0,8},{1,9},{2,10},{3,11},{4,12},{5,13},{6,14},{7,15},{8,0},{9,1},... | collective-permute-start | bytes 393224 | tf_op jit(solution)/shard_map/ppermute | solution.py:38
  289.3 7.7 %collective-permute-start.4 = (f32[32,512]{1,0:T(8,128)S(1)}, f32[32,512]{1,0:T(8,128)S(1)}, u32[]{:S(2)}, u32[]{:S(2)}) collective-permute-start(f32[32,512]{1,0:T(8,128)S(1)} %constant_dynamic-slice_fusion.6), channel_id=1, source_target_pairs={{0,16},{1,17},{2,18},{3,19},{4,20},{5,21},{6,22},{7,23},{8,24},{9,... | collective-permute-start | bytes 196616 | tf_op jit(solution)/shard_map/ppermute | solution.py:38
  297.0 5.8 %collective-permute-start.5 = (f32[16,512]{1,0:T(8,128)S(1)}, f32[16,512]{1,0:T(8,128)S(1)}, u32[]{:S(2)}, u32[]{:S(2)}) collective-permute-start(f32[16,512]{1,0:T(8,128)S(1)} %constant_dynamic-slice_fusion.5), channel_id=1, source_target_pairs={{0,32},{32,0},{64,96},{96,64},{128,160},{160,128},{192,224},{224,1... | collective-permute-start | bytes 98312 | tf_op jit(solution)/shard_map/ppermute | solution.py:38
  302.8 6.5 %collective-permute-start.6 = (f32[8,512]{1,0:T(8,128)S(1)}, f32[8,512]{1,0:T(8,128)S(1)}, u32[]{:S(2)}, u32[]{:S(2)}) collective-permute-start(f32[8,512]{1,0:T(8,128)S(1)} %constant_dynamic-slice_fusion.4), channel_id=1, source_target_pairs={{0,64},{32,96},{64,0},{96,32},{128,192},{160,224},{192,128},{224,1... | collective-permute-start | bytes 49160 | tf_op jit(solution)/shard_map/ppermute | solution.py:38
  309.3 9.5 %collective-permute-start.7 = (f32[4,512]{1,0:T(4,128)S(1)}, f32[4,512]{1,0:T(4,128)S(1)}, u32[]{:S(2)}, u32[]{:S(2)}) collective-permute-start(f32[4,512]{1,0:T(4,128)S(1)} %constant_dynamic-slice_fusion.2), channel_id=1, source_target_pairs={{0,128},{32,160},{64,192},{96,224},{128,0},{160,32},{192,64},{224,... | collective-permute-start | bytes 24584 | tf_op jit(solution)/shard_map/ppermute | solution.py:38
  318.8 14.2 %collective-permute-start.8 = (f32[2,512]{1,0:T(2,128)S(1)}, f32[2,512]{1,0:T(2,128)S(1)}, u32[]{:S(2)}, u32[]{:S(2)}) collective-permute-start(f32[2,512]{1,0:T(2,128)S(1)} %constant_dynamic-slice_fusion), channel_id=1, source_target_pairs={{0,256},{32,288},{64,320},{96,352},{128,384},{160,416},{192,448},{... | collective-permute-start | bytes 12296 | tf_op jit(solution)/shard_map/ppermute | solution.py:38
  333.0 14.2 %collective-permute-start.9 = (f32[2,512]{1,0:T(2,128)S(1)}, f32[2,512]{1,0:T(2,128)S(1)}, u32[]{:S(2)}, u32[]{:S(2)}) collective-permute-start(f32[2,512]{1,0:T(2,128)S(1)} %get-tuple-element.16), channel_id=1, source_target_pairs={{0,256},{32,288},{64,320},{96,352},{128,384},{160,416},{192,448},{... | collective-permute-start | bytes 12296 | tf_op jit(solution)/shard_map/ppermute | solution.py:44
  347.3 9.4 %collective-permute-start.10 = (f32[4,512]{1,0:T(4,128)S(1)}, f32[4,512]{1,0:T(4,128)S(1)}, u32[]{:S(2)}, u32[]{:S(2)}) collective-permute-start(f32[4,512]{1,0:T(4,128)S(1)} %constant_dynamic-update-slice_fusion.16), channel_id=1, source_target_pairs={{0,128},{32,160},{64,192},{96,224},{128,0},{160,32},{192,64},{224,... | collective-permute-start | bytes 24584 | tf_op jit(solution)/shard_map/ppermute | solution.py:44
  356.7 6.5 %collective-permute-start.11 = (f32[8,512]{1,0:T(8,128)S(1)}, f32[8,512]{1,0:T(8,128)S(1)}, u32[]{:S(2)}, u32[]{:S(2)}) collective-permute-start(f32[8,512]{1,0:T(8,128)S(1)} %constant_dynamic-update-slice_fusion.14), channel_id=1, source_target_pairs={{0,64},{32,96},{64,0},{96,32},{128,192},{160,224},{192,128},{224,1... | collective-permute-start | bytes 49160 | tf_op jit(solution)/shard_map/ppermute | solution.py:44
  363.2 5.8 %collective-permute-start.12 = (f32[16,512]{1,0:T(8,128)S(1)}, f32[16,512]{1,0:T(8,128)S(1)}, u32[]{:S(2)}, u32[]{:S(2)}) collective-permute-start(f32[16,512]{1,0:T(8,128)S(1)} %constant_dynamic-update-slice_fusion.12), channel_id=1, source_target_pairs={{0,32},{32,0},{64,96},{96,64},{128,160},{160,128},{192,224},{224,1... | collective-permute-start | bytes 98312 | tf_op jit(solution)/shard_map/ppermute | solution.py:44
  369.0 7.7 %collective-permute-start.13 = (f32[32,512]{1,0:T(8,128)S(1)}, f32[32,512]{1,0:T(8,128)S(1)}, u32[]{:S(2)}, u32[]{:S(2)}) collective-permute-start(f32[32,512]{1,0:T(8,128)S(1)} %constant_dynamic-update-slice_fusion.10), channel_id=1, source_target_pairs={{0,16},{1,17},{2,18},{3,19},{4,20},{5,21},{6,22},{7,23},{8,24},{9,... | collective-permute-start | bytes 196616 | tf_op jit(solution)/shard_map/ppermute | solution.py:44
  376.7 6.9 %collective-permute-start.14 = (f32[64,512]{1,0:T(8,128)S(1)}, f32[64,512]{1,0:T(8,128)S(1)}, u32[]{:S(2)}, u32[]{:S(2)}) collective-permute-start(f32[64,512]{1,0:T(8,128)S(1)} %constant_dynamic-update-slice_fusion.8), channel_id=1, source_target_pairs={{0,8},{1,9},{2,10},{3,11},{4,12},{5,13},{6,14},{7,15},{8,0},{9,1},... | collective-permute-start | bytes 393224 | tf_op jit(solution)/shard_map/ppermute | solution.py:44
  383.6 9.8 %collective-permute-start.15 = (f32[128,512]{1,0:T(8,128)S(1)}, f32[128,512]{1,0:T(8,128)S(1)}, u32[]{:S(2)}, u32[]{:S(2)}) collective-permute-start(f32[128,512]{1,0:T(8,128)S(1)} %constant_dynamic-update-slice_fusion.6), channel_id=1, source_target_pairs={{0,4},{1,5},{2,6},{3,7},{4,0},{5,1},{6,2},{7,3},{8,12},{9,13},{10,... | collective-permute-start | bytes 786440 | tf_op jit(solution)/shard_map/ppermute | solution.py:44
  393.4 11.1 %collective-permute-start.16 = (f32[256,512]{1,0:T(8,128)S(1)}, f32[256,512]{1,0:T(8,128)S(1)}, u32[]{:S(2)}, u32[]{:S(2)}) collective-permute-start(f32[256,512]{1,0:T(8,128)S(1)} %constant_dynamic-update-slice_fusion.4), channel_id=1, source_target_pairs={{0,2},{1,3},{2,0},{3,1},{4,6},{5,7},{6,4},{7,5},{8,10},{9,11},{10,... | collective-permute-start | bytes 1572872 | tf_op jit(solution)/shard_map/ppermute | solution.py:44
  404.5 67.8 %collective-permute-start.17 = (f32[512,512]{1,0:T(8,128)S(1)}, f32[512,512]{1,0:T(8,128)S(1)}, u32[]{:S(2)}, u32[]{:S(2)}) collective-permute-start(f32[512,512]{1,0:T(8,128)S(1)} %constant_dynamic-update-slice_fusion.2), channel_id=1, source_target_pairs={{0,1},{1,0},{2,3},{3,2},{4,5},{5,4},{6,7},{7,6},{8,9},{9,8},{10,11... | collective-permute-start | bytes 3145736 | tf_op jit(solution)/shard_map/ppermute | solution.py:44
  407.7 3.2 collective-permute-start.18
  410.9 5.5 %collective-permute-start.19 = (f32[8,128]{1,0:T(8,128)S(1)}, f32[8,128]{1,0:T(8,128)S(1)}, u32[]{:S(2)}, u32[]{:S(2)}) collective-permute-start(f32[8,128]{1,0:T(8,128)S(1)} %broadcast_add_fusion), channel_id=1, source_target_pairs={{0,2},{1,3},{2,0},{3,1},{4,6},{5,7},{6,4},{7,5},{8,10},{9,11},{10,... | collective-permute-start | bytes 12296 | tf_op jit(solution)/shard_map/ppermute | solution.py:38
  416.4 7.0 %collective-permute-start.20 = (f32[8,128]{1,0:T(8,128)S(1)}, f32[8,128]{1,0:T(8,128)S(1)}, u32[]{:S(2)}, u32[]{:S(2)}) collective-permute-start(f32[8,128]{1,0:T(8,128)S(1)} %fusion.56), channel_id=1, source_target_pairs={{0,4},{1,5},{2,6},{3,7},{4,0},{5,1},{6,2},{7,3},{8,12},{9,13},{10,... | collective-permute-start | bytes 12296 | tf_op jit(solution)/shard_map/ppermute | solution.py:38
  423.4 5.5 %collective-permute-start.21 = (f32[8,128]{1,0:T(8,128)S(1)}, f32[8,128]{1,0:T(8,128)S(1)}, u32[]{:S(2)}, u32[]{:S(2)}) collective-permute-start(f32[8,128]{1,0:T(8,128)S(1)} %add.273), channel_id=1, source_target_pairs={{0,8},{1,9},{2,10},{3,11},{4,12},{5,13},{6,14},{7,15},{8,0},{9,1},... | collective-permute-start | bytes 12296 | tf_op jit(solution)/shard_map/ppermute | solution.py:38
  428.9 7.0 %collective-permute-start.22 = (f32[8,128]{1,0:T(8,128)S(1)}, f32[8,128]{1,0:T(8,128)S(1)}, u32[]{:S(2)}, u32[]{:S(2)}) collective-permute-start(f32[8,128]{1,0:T(8,128)S(1)} %add.274), channel_id=1, source_target_pairs={{0,16},{1,17},{2,18},{3,19},{4,20},{5,21},{6,22},{7,23},{8,24},{9,... | collective-permute-start | bytes 12296 | tf_op jit(solution)/shard_map/ppermute | solution.py:38
  435.9 5.5 %collective-permute-start.23 = (f32[8,128]{1,0:T(8,128)S(1)}, f32[8,128]{1,0:T(8,128)S(1)}, u32[]{:S(2)}, u32[]{:S(2)}) collective-permute-start(f32[8,128]{1,0:T(8,128)S(1)} %add.275), channel_id=1, source_target_pairs={{0,32},{32,0},{64,96},{96,64},{128,160},{160,128},{192,224},{224,1... | collective-permute-start | bytes 12296 | tf_op jit(solution)/shard_map/ppermute | solution.py:38
  441.4 6.4 %collective-permute-start.24 = (f32[8,128]{1,0:T(8,128)S(1)}, f32[8,128]{1,0:T(8,128)S(1)}, u32[]{:S(2)}, u32[]{:S(2)}) collective-permute-start(f32[8,128]{1,0:T(8,128)S(1)} %add.276), channel_id=1, source_target_pairs={{0,64},{32,96},{64,0},{96,32},{128,192},{160,224},{192,128},{224,1... | collective-permute-start | bytes 12296 | tf_op jit(solution)/shard_map/ppermute | solution.py:38
  447.8 9.4 %collective-permute-start.25 = (f32[8,128]{1,0:T(8,128)S(1)}, f32[8,128]{1,0:T(8,128)S(1)}, u32[]{:S(2)}, u32[]{:S(2)}) collective-permute-start(f32[8,128]{1,0:T(8,128)S(1)} %add.277), channel_id=1, source_target_pairs={{0,128},{32,160},{64,192},{96,224},{128,0},{160,32},{192,64},{224,... | collective-permute-start | bytes 12296 | tf_op jit(solution)/shard_map/ppermute | solution.py:38
  457.2 14.2 %collective-permute-start.26 = (f32[8,128]{1,0:T(8,128)S(1)}, f32[8,128]{1,0:T(8,128)S(1)}, u32[]{:S(2)}, u32[]{:S(2)}) collective-permute-start(f32[8,128]{1,0:T(8,128)S(1)} %add.278), channel_id=1, source_target_pairs={{0,256},{32,288},{64,320},{96,352},{128,384},{160,416},{192,448},{... | collective-permute-start | bytes 12296 | tf_op jit(solution)/shard_map/ppermute | solution.py:38
Sparse Core Ops, SparseCore 0:
  11.2 65.5 all-gather.3
  86.5 78.5 all-gather.5
  168.5 69.4 all-gather.7
where the time goes:
time: 482 us; the launch traced here: 480 us
  waiting for transfers between devices  316 us (66%)
  starting transfers between devices  113 us (23%)
  matrix products  19.9 us (4%)
  between operations  16.7 us (3%)
  local copies, waits for them, and re-layouts  9.08 us (2%)
  other arithmetic  6.42 us (1%)
    all_gather x1, waiting for transfers between devices, body(): candidates = lax.all_gather(zeta_bf[:NOISE], 'row', axis=0, tiled=True)  77.2 us
    ppermute x18, starting transfers between devices, tree_allreduce(): got, got_extra = lax.ppermute((send, extra), axis, xor_pairs(size, mask))  75.2 us
    ppermute x18, waiting for transfers between devices, tree_allreduce(): got, got_extra = lax.ppermute((send, extra), axis, xor_pairs(size, mask))  70.2 us
    all_gather x1, waiting for transfers between devices, body(): piece = lax.all_gather(source_feats, 'col', axis=0, tiled=True)  66.5 us
    all_gather x1, waiting for transfers between devices, body(): lax.all_gather(dnoise.astype(jnp.bfloat16), 'row', axis=0, tiled=True)  65.5 us
    ppermute x9, starting transfers between devices, tree_allreduce(): got = lax.ppermute(buf, axis, xor_pairs(size, mask))  37.3 us
    ppermute x9, waiting for transfers between devices, tree_allreduce(): got = lax.ppermute(buf, axis, xor_pairs(size, mask))  35.4 us
  transfers between devices with their start and end apart: 30, of which 29 were waited for; matrix products, arithmetic and copies ran while one was open for 2% of the time, Pallas kernels for 0%

commit v1 on v0

--- a/solution.py
+++ b/solution.py
@@ -73,7 +73,10 @@
     scale_factor = 1.0 / softness_divisor
     valid = jnp.arange(slots, dtype=jnp.int32)[None, :] < nbr_count[:, None]
     tiles = adj_tiles * valid[:, :, None, None].astype(jnp.bfloat16)
-    piece = lax.all_gather(source_feats, "col", axis=0, tiled=True)
+    n_dev = lax.axis_size("col")
+    shards = jnp.stack([source_feats for _ in range(n_dev)])
+    shards = lax.all_to_all(shards, "col", split_axis=0, concat_axis=0)
+    piece = jnp.concatenate(shards, axis=0)
     count = piece.shape[0] // BLOCK
     blocks = piece.reshape(count, BLOCK, width)
     indicator_matrix = (

time: 482 us -> 477 us (0.990)
  waiting for transfers between devices: 316 us -> 298 us
  starting transfers between devices: 113 us -> 123 us
    all_gather x1 -> x0, waiting for transfers between devices: 66.5 us -> none  [body(): piece = lax.all_gather(source_feats, 'col', axis=0, tiled=True)]
    all_to_all x0 -> x1, waiting for transfers between devices: none -> 50.8 us  [body(): shards = lax.all_to_all(shards, 'col', split_axis=0, concat_axis=0)]
    all_to_all x0 -> x1, starting transfers between devices: none -> 10.5 us  [body(): shards = lax.all_to_all(shards, 'col', split_axis=0, concat_axis=0)]
  transfers between devices with their start and end apart: 30 -> 30, of which waited for: 29 -> 29; matrix products, arithmetic and copies ran while one was open for 2% -> 1% of each run, Pallas kernels for 0% -> 0%
where the time goes in v1:
time: 477 us; the launch traced here: 476 us
  waiting for transfers between devices  298 us (62%)
  starting transfers between devices  123 us (26%)
  matrix products  18.8 us (4%)
  between operations  17 us (4%)
  local copies, waits for them, and re-layouts  12.6 us (3%)
  other arithmetic  5.77 us (1%)
    all_gather x1, waiting for transfers between devices, body(): candidates = lax.all_gather(zeta_bf[:NOISE], 'row', axis=0, tiled=True)  76.4 us
    ppermute x18, starting transfers between devices, tree_allreduce(): got, got_extra = lax.ppermute((send, extra), axis, xor_pairs(size, mask))  75.2 us
    ppermute x18, waiting for transfers between devices, tree_allreduce(): got, got_extra = lax.ppermute((send, extra), axis, xor_pairs(size, mask))  70.2 us
    all_gather x1, waiting for transfers between devices, body(): lax.all_gather(dnoise.astype(jnp.bfloat16), 'row', axis=0, tiled=True)  65.6 us
    all_to_all x1, waiting for transfers between devices, body(): shards = lax.all_to_all(shards, 'col', split_axis=0, concat_axis=0)  50.8 us
    ppermute x9, starting transfers between devices, tree_allreduce(): got = lax.ppermute(buf, axis, xor_pairs(size, mask))  37.3 us
    ppermute x9, waiting for transfers between devices, tree_allreduce(): got = lax.ppermute(buf, axis, xor_pairs(size, mask))  35.4 us
    all_to_all x1, starting transfers between devices, body(): shards = lax.all_to_all(shards, 'col', split_axis=0, concat_axis=0)  10.5 us
  transfers between devices with their start and end apart: 30, of which 29 were waited for; matrix products, arithmetic and copies ran while one was open for 1% of the time, Pallas kernels for 0%

profile of v1, /device:TPU:2, one launch (start us, length us, event | category | flops | bytes accessed | tf_op | source)
XLA Modules:
  0.0 475.8 jit_solution(15777186208036326693)
XLA Ops:
  7.2 3.5 stack.2
  10.6 10.5 %all-to-all-start = ((bf16[32,128,512]{2,1,0:T(8,128)(2,1)}), bf16[32,128,512]{2,1,0:T(8,128)(2,1)}, u32[]{:S(2)}, u32[]{:S(2)}) async-start(bf16[32,128,512]{2,1,0:T(8,128)(2,1)} %stack.2), calls=%async_computation | async-start | bytes 8388608 | tf_op jit(solution)/shard_map/all_to_all | solution.py:78
  21.8 50.8 %all-to-all-done = bf16[32,128,512]{2,1,0:T(8,128)(2,1)} async-done(((bf16[32,128,512]{2,1,0:T(8,128)(2,1)}), bf16[32,128,512]{2,1,0:T(8,128)(2,1)}, u32[]{:S(2)}, u32[]{:S(2)}) %all-to-all-start) | async-done | bytes 4194336 | tf_op jit(solution)/shard_map/all_to_all | solution.py:78
  72.6 5.5 %fusion.1 = bf16[4,8,128,512]{3,1,2,0:T(8,128)(2,1)S(1)} fusion(bf16[32,128,512,1]{2,1,0,3:T(8,128)(2,1)} %bitcast.2, s32[4,8]{1,0:T(4,128)S(1)} %copy-done.6), kind=kOutput, calls=%fused_computation.2 | convolution fusion | flops 134218752 | bytes 8388736 | tf_op jit(solution)/shard_map/bkc,cjd->bkjd/dot_general | solution.py:85
  78.2 2.6 fusion.8
  83.8 76.4 %all-gather.3.cloned.1.call-done = bf16[2048,512]{0,1:T(8,128)(2,1)} async-done(((bf16[128,512]{0,1:T(8,128)(2,1)}), bf16[2048,512]{0,1:T(8,128)(2,1)}) %all-gather.3.cloned.1.call-update) | async-done | bytes 2097168 | tf_op jit(solution)/shard_map/all_gather | solution.py:95
  160.1 1.9 fusion.21
  164.7 1.6 fusion.7
  167.5 65.6 %all-gather.5.cloned.1.call-done = bf16[2048,512]{1,0:T(8,128)(2,1)} async-done(((bf16[128,512]{1,0:T(8,128)(2,1)}), bf16[2048,512]{1,0:T(8,128)(2,1)}) %all-gather.5.cloned.1.call-update) | async-done | bytes 2097168 | tf_op jit(solution)/shard_map/all_gather | solution.py:113
  233.1 3.2 reshape.97
  236.3 2.0 fusion.3
  241.9 1.9 collective-permute-start
  243.9 2.9 collective-permute-done
  246.8 1.7 fusion.14
  249.5 2.5 collective-permute-start.1
  252.0 13.3 %collective-permute-done.1 = f32[256,512]{1,0:T(8,128)S(1)} collective-permute-done((f32[256,512]{1,0:T(8,128)S(1)}, f32[256,512]{1,0:T(8,128)S(1)}, u32[]{:S(2)}, u32[]{:S(2)}) %collective-permute-start.1) | collective-permute-done | bytes 524320 | tf_op jit(solution)/shard_map/ppermute | solution.py:38
  266.5 4.0 collective-permute-start.2
  270.5 6.9 %collective-permute-done.2 = f32[128,512]{1,0:T(8,128)S(1)} collective-permute-done((f32[128,512]{1,0:T(8,128)S(1)}, f32[128,512]{1,0:T(8,128)S(1)}, u32[]{:S(2)}, u32[]{:S(2)}) %collective-permute-start.2) | collective-permute-done | bytes 262176 | tf_op jit(solution)/shard_map/ppermute | solution.py:38
  277.5 3.4 collective-permute-start.3
  280.9 3.4 collective-permute-done.3
  284.4 4.9 %collective-permute-start.4 = (f32[32,512]{1,0:T(8,128)S(1)}, f32[32,512]{1,0:T(8,128)S(1)}, u32[]{:S(2)}, u32[]{:S(2)}) collective-permute-start(f32[32,512]{1,0:T(8,128)S(1)} %constant_dynamic-slice_fusion.6), channel_id=1, source_target_pairs={{0,16},{1,17},{2,18},{3,19},{4,20},{5,21},{6,22},{7,23},{8,24},{9,... | collective-permute-start | bytes 196616 | tf_op jit(solution)/shard_map/ppermute | solution.py:38
  289.3 2.7 collective-permute-done.4
  292.1 3.6 collective-permute-start.5
  295.7 2.2 collective-permute-done.5
  297.9 3.4 collective-permute-start.6
  301.3 3.1 collective-permute-done.6
  304.4 5.1 %collective-permute-start.7 = (f32[4,512]{1,0:T(4,128)S(1)}, f32[4,512]{1,0:T(4,128)S(1)}, u32[]{:S(2)}, u32[]{:S(2)}) collective-permute-start(f32[4,512]{1,0:T(4,128)S(1)} %constant_dynamic-slice_fusion.2), channel_id=1, source_target_pairs={{0,128},{32,160},{64,192},{96,224},{128,0},{160,32},{192,64},{224,... | collective-permute-start | bytes 24584 | tf_op jit(solution)/shard_map/ppermute | solution.py:38
  309.6 4.3 collective-permute-done.7
  313.9 8.6 %collective-permute-start.8 = (f32[2,512]{1,0:T(2,128)S(1)}, f32[2,512]{1,0:T(2,128)S(1)}, u32[]{:S(2)}, u32[]{:S(2)}) collective-permute-start(f32[2,512]{1,0:T(2,128)S(1)} %constant_dynamic-slice_fusion), channel_id=1, source_target_pairs={{0,256},{32,288},{64,320},{96,352},{128,384},{160,416},{192,448},{... | collective-permute-start | bytes 12296 | tf_op jit(solution)/shard_map/ppermute | solution.py:38
  322.6 5.6 %collective-permute-done.8 = f32[2,512]{1,0:T(2,128)S(1)} collective-permute-done((f32[2,512]{1,0:T(2,128)S(1)}, f32[2,512]{1,0:T(2,128)S(1)}, u32[]{:S(2)}, u32[]{:S(2)}) %collective-permute-start.8) | collective-permute-done | bytes 4128 | tf_op jit(solution)/shard_map/ppermute | solution.py:38
  328.1 8.6 %collective-permute-start.9 = (f32[2,512]{1,0:T(2,128)S(1)}, f32[2,512]{1,0:T(2,128)S(1)}, u32[]{:S(2)}, u32[]{:S(2)}) collective-permute-start(f32[2,512]{1,0:T(2,128)S(1)} %get-tuple-element.16), channel_id=1, source_target_pairs={{0,256},{32,288},{64,320},{96,352},{128,384},{160,416},{192,448},{... | collective-permute-start | bytes 12296 | tf_op jit(solution)/shard_map/ppermute | solution.py:44
  336.8 5.6 %collective-permute-done.9 = f32[2,512]{1,0:T(2,128)S(1)} collective-permute-done((f32[2,512]{1,0:T(2,128)S(1)}, f32[2,512]{1,0:T(2,128)S(1)}, u32[]{:S(2)}, u32[]{:S(2)}) %collective-permute-start.9) | collective-permute-done | bytes 4128 | tf_op jit(solution)/shard_map/ppermute | solution.py:44
  342.4 5.1 %collective-permute-start.10 = (f32[4,512]{1,0:T(4,128)S(1)}, f32[4,512]{1,0:T(4,128)S(1)}, u32[]{:S(2)}, u32[]{:S(2)}) collective-permute-start(f32[4,512]{1,0:T(4,128)S(1)} %constant_dynamic-update-slice_fusion.16), channel_id=1, source_target_pairs={{0,128},{32,160},{64,192},{96,224},{128,0},{160,32},{192,64},{224,... | collective-permute-start | bytes 24584 | tf_op jit(solution)/shard_map/ppermute | solution.py:44
  347.5 4.3 collective-permute-done.10
  351.8 3.4 collective-permute-start.11
  355.2 3.1 collective-permute-done.11
  358.3 3.6 collective-permute-start.12
  362.0 2.2 collective-permute-done.12
  364.1 4.9 %collective-permute-start.13 = (f32[32,512]{1,0:T(8,128)S(1)}, f32[32,512]{1,0:T(8,128)S(1)}, u32[]{:S(2)}, u32[]{:S(2)}) collective-permute-start(f32[32,512]{1,0:T(8,128)S(1)} %constant_dynamic-update-slice_fusion.10), channel_id=1, source_target_pairs={{0,16},{1,17},{2,18},{3,19},{4,20},{5,21},{6,22},{7,23},{8,24},{9,... | collective-permute-start | bytes 196616 | tf_op jit(solution)/shard_map/ppermute | solution.py:44
  369.1 2.7 collective-permute-done.13
  371.8 3.4 collective-permute-start.14
  375.3 3.4 collective-permute-done.14
  378.7 4.0 collective-permute-start.15
  382.8 5.7 %collective-permute-done.15 = f32[128,512]{1,0:T(8,128)S(1)} collective-permute-done((f32[128,512]{1,0:T(8,128)S(1)}, f32[128,512]{1,0:T(8,128)S(1)}, u32[]{:S(2)}, u32[]{:S(2)}) %collective-permute-start.15) | collective-permute-done | bytes 262176 | tf_op jit(solution)/shard_map/ppermute | solution.py:44
  388.5 2.5 collective-permute-start.16
  391.1 8.4 %collective-permute-done.16 = f32[256,512]{1,0:T(8,128)S(1)} collective-permute-done((f32[256,512]{1,0:T(8,128)S(1)}, f32[256,512]{1,0:T(8,128)S(1)}, u32[]{:S(2)}, u32[]{:S(2)}) %collective-permute-start.16) | collective-permute-done | bytes 524320 | tf_op jit(solution)/shard_map/ppermute | solution.py:44
  399.6 1.9 collective-permute-start.17
  402.8 2.4 collective-permute-start.18
  406.1 2.5 collective-permute-start.19
  408.5 3.0 collective-permute-done.19
  411.5 4.0 collective-permute-start.20
  415.5 3.0 collective-permute-done.20
  418.5 3.4 collective-permute-start.21
  421.9 2.1 collective-permute-done.21
  424.0 4.9 %collective-permute-start.22 = (f32[8,128]{1,0:T(8,128)S(1)}, f32[8,128]{1,0:T(8,128)S(1)}, u32[]{:S(2)}, u32[]{:S(2)}) collective-permute-start(f32[8,128]{1,0:T(8,128)S(1)} %add.274), channel_id=1, source_target_pairs={{0,16},{1,17},{2,18},{3,19},{4,20},{5,21},{6,22},{7,23},{8,24},{9,... | collective-permute-start | bytes 12296 | tf_op jit(solution)/shard_map/ppermute | solution.py:38
  429.0 2.1 collective-permute-done.22
  431.0 3.6 collective-permute-start.23
  434.6 1.9 collective-permute-done.23
  436.5 3.4 collective-permute-start.24
  439.9 3.0 collective-permute-done.24
  442.9 5.1 %collective-permute-start.25 = (f32[8,128]{1,0:T(8,128)S(1)}, f32[8,128]{1,0:T(8,128)S(1)}, u32[]{:S(2)}, u32[]{:S(2)}) collective-permute-start(f32[8,128]{1,0:T(8,128)S(1)} %add.277), channel_id=1, source_target_pairs={{0,128},{32,160},{64,192},{96,224},{128,0},{160,32},{192,64},{224,... | collective-permute-start | bytes 12296 | tf_op jit(solution)/shard_map/ppermute | solution.py:38
  448.0 4.3 collective-permute-done.25
  452.3 8.7 %collective-permute-start.26 = (f32[8,128]{1,0:T(8,128)S(1)}, f32[8,128]{1,0:T(8,128)S(1)}, u32[]{:S(2)}, u32[]{:S(2)}) collective-permute-start(f32[8,128]{1,0:T(8,128)S(1)} %add.278), channel_id=1, source_target_pairs={{0,256},{32,288},{64,320},{96,352},{128,384},{160,416},{192,448},{... | collective-permute-start | bytes 12296 | tf_op jit(solution)/shard_map/ppermute | solution.py:38
  461.0 5.5 %collective-permute-done.26 = f32[8,128]{1,0:T(8,128)S(1)} collective-permute-done((f32[8,128]{1,0:T(8,128)S(1)}, f32[8,128]{1,0:T(8,128)S(1)}, u32[]{:S(2)}, u32[]{:S(2)}) %collective-permute-start.26) | collective-permute-done | bytes 4128 | tf_op jit(solution)/shard_map/ppermute | solution.py:38
  (101 shorter events, 16.3 us)
Async XLA Ops:
  7.2 14.1 %copy-start = (bf16[512,512]{1,0:T(8,128)(2,1)S(1)}, bf16[512,512]{1,0:T(8,128)(2,1)}, u32[]{:S(2)}) copy-start(bf16[512,512]{1,0:T(8,128)(2,1)} %param.11) | copy-start | bytes 1572868
  10.6 10.6 %copy-start.10 = (s32[4]{0:T(128)S(1)}, s32[4]{0:T(128)}, u32[]{:S(2)}) copy-start(s32[4]{0:T(128)} %param.14) | copy-start | bytes 52
  10.6 10.6 %copy-start.4 = (bf16[512,512]{1,0:T(8,128)(2,1)S(1)}, bf16[512,512]{1,0:T(8,128)(2,1)}, u32[]{:S(2)}) copy-start(bf16[512,512]{1,0:T(8,128)(2,1)} %param.18) | copy-start | bytes 1572868
  10.6 62.0 %all-to-all-start = ((bf16[32,128,512]{2,1,0:T(8,128)(2,1)}), bf16[32,128,512]{2,1,0:T(8,128)(2,1)}, u32[]{:S(2)}, u32[]{:S(2)}) async-start(bf16[32,128,512]{2,1,0:T(8,128)(2,1)} %stack.2), calls=%async_computation | async-start | bytes 8388608 | tf_op jit(solution)/shard_map/all_to_all | solution.py:78
  21.1 51.5 %copy-start.6 = (s32[4,8]{1,0:T(4,128)S(1)}, s32[4,8]{1,0:T(4,128)}, u32[]{:S(2)}) copy-start(s32[4,8]{1,0:T(4,128)} %param.13) | copy-start | bytes 388
  21.1 139.0 %all-gather.3.cloned.1.call-start = ((), (), s32[]{:S(2)}) async-start(), calls=%async_computation.1 | async-start | bytes 2228224 | tf_op jit(solution)/shard_map/all_gather | solution.py:95
  72.6 5.5 %copy-start.9 = (bf16[4,8,128,128]{3,2,1,0:T(8,128)(2,1)S(1)}, bf16[4,8,128,128]{3,2,1,0:T(8,128)(2,1)}, u32[]{:S(2)}) copy-start(bf16[4,8,128,128]{3,2,1,0:T(8,128)(2,1)} %param.15) | copy-start | bytes 3145732
  78.2 2.6 copy-start.5
  80.8 0.8 copy-start.2
  80.8 1.7 copy-start.8
  81.6 81.9 %copy-start.7 = (s32[512]{0:T(512)S(1)}, s32[512]{0:T(512)}, u32[]{:S(2)}) copy-start(s32[512]{0:T(512)} %param.16) | copy-start | bytes 6148
  82.3 150.8 %all-gather.5.cloned.1.call-start = ((), (), s32[]{:S(2)}) async-start(), calls=%async_computation.2 | async-start | bytes 2228224 | tf_op jit(solution)/shard_map/all_gather | solution.py:113
  238.5 1.0 copy-start.3
  241.9 4.9 %collective-permute-start = (f32[512,512]{1,0:T(8,128)}, f32[512,512]{1,0:T(8,128)}, u32[]{:S(2)}, u32[]{:S(2)}) collective-permute-start(f32[512,512]{1,0:T(8,128)} %fusion.12), channel_id=1, source_target_pairs={{0,1},{1,0},{2,3},{3,2},{4,5},{5,4},{6,7},{7,6},{8,9},{9,8},{10,11... | collective-permute-start | bytes 3145736 | tf_op jit(solution)/shard_map/ppermute | solution.py:38
  248.5 1.0 copy-start.1
  249.5 15.9 %collective-permute-start.1 = (f32[256,512]{1,0:T(8,128)S(1)}, f32[256,512]{1,0:T(8,128)S(1)}, u32[]{:S(2)}, u32[]{:S(2)}) collective-permute-start(f32[256,512]{1,0:T(8,128)S(1)} %constant_dynamic-slice_fusion.9), channel_id=1, source_target_pairs={{0,2},{1,3},{2,0},{3,1},{4,6},{5,7},{6,4},{7,5},{8,10},{9,11},{10,... | collective-permute-start | bytes 1572872 | tf_op jit(solution)/shard_map/ppermute | solution.py:38
  266.5 10.9 %collective-permute-start.2 = (f32[128,512]{1,0:T(8,128)S(1)}, f32[128,512]{1,0:T(8,128)S(1)}, u32[]{:S(2)}, u32[]{:S(2)}) collective-permute-start(f32[128,512]{1,0:T(8,128)S(1)} %constant_dynamic-slice_fusion.8), channel_id=1, source_target_pairs={{0,4},{1,5},{2,6},{3,7},{4,0},{5,1},{6,2},{7,3},{8,12},{9,13},{10,... | collective-permute-start | bytes 786440 | tf_op jit(solution)/shard_map/ppermute | solution.py:38
  277.5 6.9 %collective-permute-start.3 = (f32[64,512]{1,0:T(8,128)S(1)}, f32[64,512]{1,0:T(8,128)S(1)}, u32[]{:S(2)}, u32[]{:S(2)}) collective-permute-start(f32[64,512]{1,0:T(8,128)S(1)} %constant_dynamic-slice_fusion.7), channel_id=1, source_target_pairs={{0,8},{1,9},{2,10},{3,11},{4,12},{5,13},{6,14},{7,15},{8,0},{9,1},... | collective-permute-start | bytes 393224 | tf_op jit(solution)/shard_map/ppermute | solution.py:38
  284.4 7.7 %collective-permute-start.4 = (f32[32,512]{1,0:T(8,128)S(1)}, f32[32,512]{1,0:T(8,128)S(1)}, u32[]{:S(2)}, u32[]{:S(2)}) collective-permute-start(f32[32,512]{1,0:T(8,128)S(1)} %constant_dynamic-slice_fusion.6), channel_id=1, source_target_pairs={{0,16},{1,17},{2,18},{3,19},{4,20},{5,21},{6,22},{7,23},{8,24},{9,... | collective-permute-start | bytes 196616 | tf_op jit(solution)/shard_map/ppermute | solution.py:38
  292.1 5.8 %collective-permute-start.5 = (f32[16,512]{1,0:T(8,128)S(1)}, f32[16,512]{1,0:T(8,128)S(1)}, u32[]{:S(2)}, u32[]{:S(2)}) collective-permute-start(f32[16,512]{1,0:T(8,128)S(1)} %constant_dynamic-slice_fusion.5), channel_id=1, source_target_pairs={{0,32},{32,0},{64,96},{96,64},{128,160},{160,128},{192,224},{224,1... | collective-permute-start | bytes 98312 | tf_op jit(solution)/shard_map/ppermute | solution.py:38
  297.9 6.5 %collective-permute-start.6 = (f32[8,512]{1,0:T(8,128)S(1)}, f32[8,512]{1,0:T(8,128)S(1)}, u32[]{:S(2)}, u32[]{:S(2)}) collective-permute-start(f32[8,512]{1,0:T(8,128)S(1)} %constant_dynamic-slice_fusion.4), channel_id=1, source_target_pairs={{0,64},{32,96},{64,0},{96,32},{128,192},{160,224},{192,128},{224,1... | collective-permute-start | bytes 49160 | tf_op jit(solution)/shard_map/ppermute | solution.py:38
  304.4 9.5 %collective-permute-start.7 = (f32[4,512]{1,0:T(4,128)S(1)}, f32[4,512]{1,0:T(4,128)S(1)}, u32[]{:S(2)}, u32[]{:S(2)}) collective-permute-start(f32[4,512]{1,0:T(4,128)S(1)} %constant_dynamic-slice_fusion.2), channel_id=1, source_target_pairs={{0,128},{32,160},{64,192},{96,224},{128,0},{160,32},{192,64},{224,... | collective-permute-start | bytes 24584 | tf_op jit(solution)/shard_map/ppermute | solution.py:38
  313.9 14.2 %collective-permute-start.8 = (f32[2,512]{1,0:T(2,128)S(1)}, f32[2,512]{1,0:T(2,128)S(1)}, u32[]{:S(2)}, u32[]{:S(2)}) collective-permute-start(f32[2,512]{1,0:T(2,128)S(1)} %constant_dynamic-slice_fusion), channel_id=1, source_target_pairs={{0,256},{32,288},{64,320},{96,352},{128,384},{160,416},{192,448},{... | collective-permute-start | bytes 12296 | tf_op jit(solution)/shard_map/ppermute | solution.py:38
  328.1 14.2 %collective-permute-start.9 = (f32[2,512]{1,0:T(2,128)S(1)}, f32[2,512]{1,0:T(2,128)S(1)}, u32[]{:S(2)}, u32[]{:S(2)}) collective-permute-start(f32[2,512]{1,0:T(2,128)S(1)} %get-tuple-element.16), channel_id=1, source_target_pairs={{0,256},{32,288},{64,320},{96,352},{128,384},{160,416},{192,448},{... | collective-permute-start | bytes 12296 | tf_op jit(solution)/shard_map/ppermute | solution.py:44
  342.4 9.4 %collective-permute-start.10 = (f32[4,512]{1,0:T(4,128)S(1)}, f32[4,512]{1,0:T(4,128)S(1)}, u32[]{:S(2)}, u32[]{:S(2)}) collective-permute-start(f32[4,512]{1,0:T(4,128)S(1)} %constant_dynamic-update-slice_fusion.16), channel_id=1, source_target_pairs={{0,128},{32,160},{64,192},{96,224},{128,0},{160,32},{192,64},{224,... | collective-permute-start | bytes 24584 | tf_op jit(solution)/shard_map/ppermute | solution.py:44
  351.8 6.5 %collective-permute-start.11 = (f32[8,512]{1,0:T(8,128)S(1)}, f32[8,512]{1,0:T(8,128)S(1)}, u32[]{:S(2)}, u32[]{:S(2)}) collective-permute-start(f32[8,512]{1,0:T(8,128)S(1)} %constant_dynamic-update-slice_fusion.14), channel_id=1, source_target_pairs={{0,64},{32,96},{64,0},{96,32},{128,192},{160,224},{192,128},{224,1... | collective-permute-start | bytes 49160 | tf_op jit(solution)/shard_map/ppermute | solution.py:44
  358.3 5.8 %collective-permute-start.12 = (f32[16,512]{1,0:T(8,128)S(1)}, f32[16,512]{1,0:T(8,128)S(1)}, u32[]{:S(2)}, u32[]{:S(2)}) collective-permute-start(f32[16,512]{1,0:T(8,128)S(1)} %constant_dynamic-update-slice_fusion.12), channel_id=1, source_target_pairs={{0,32},{32,0},{64,96},{96,64},{128,160},{160,128},{192,224},{224,1... | collective-permute-start | bytes 98312 | tf_op jit(solution)/shard_map/ppermute | solution.py:44
  364.1 7.7 %collective-permute-start.13 = (f32[32,512]{1,0:T(8,128)S(1)}, f32[32,512]{1,0:T(8,128)S(1)}, u32[]{:S(2)}, u32[]{:S(2)}) collective-permute-start(f32[32,512]{1,0:T(8,128)S(1)} %constant_dynamic-update-slice_fusion.10), channel_id=1, source_target_pairs={{0,16},{1,17},{2,18},{3,19},{4,20},{5,21},{6,22},{7,23},{8,24},{9,... | collective-permute-start | bytes 196616 | tf_op jit(solution)/shard_map/ppermute | solution.py:44
  371.8 6.9 %collective-permute-start.14 = (f32[64,512]{1,0:T(8,128)S(1)}, f32[64,512]{1,0:T(8,128)S(1)}, u32[]{:S(2)}, u32[]{:S(2)}) collective-permute-start(f32[64,512]{1,0:T(8,128)S(1)} %constant_dynamic-update-slice_fusion.8), channel_id=1, source_target_pairs={{0,8},{1,9},{2,10},{3,11},{4,12},{5,13},{6,14},{7,15},{8,0},{9,1},... | collective-permute-start | bytes 393224 | tf_op jit(solution)/shard_map/ppermute | solution.py:44
  378.7 9.8 %collective-permute-start.15 = (f32[128,512]{1,0:T(8,128)S(1)}, f32[128,512]{1,0:T(8,128)S(1)}, u32[]{:S(2)}, u32[]{:S(2)}) collective-permute-start(f32[128,512]{1,0:T(8,128)S(1)} %constant_dynamic-update-slice_fusion.6), channel_id=1, source_target_pairs={{0,4},{1,5},{2,6},{3,7},{4,0},{5,1},{6,2},{7,3},{8,12},{9,13},{10,... | collective-permute-start | bytes 786440 | tf_op jit(solution)/shard_map/ppermute | solution.py:44
  388.5 11.1 %collective-permute-start.16 = (f32[256,512]{1,0:T(8,128)S(1)}, f32[256,512]{1,0:T(8,128)S(1)}, u32[]{:S(2)}, u32[]{:S(2)}) collective-permute-start(f32[256,512]{1,0:T(8,128)S(1)} %constant_dynamic-update-slice_fusion.4), channel_id=1, source_target_pairs={{0,2},{1,3},{2,0},{3,1},{4,6},{5,7},{6,4},{7,5},{8,10},{9,11},{10,... | collective-permute-start | bytes 1572872 | tf_op jit(solution)/shard_map/ppermute | solution.py:44
  399.6 67.8 %collective-permute-start.17 = (f32[512,512]{1,0:T(8,128)S(1)}, f32[512,512]{1,0:T(8,128)S(1)}, u32[]{:S(2)}, u32[]{:S(2)}) collective-permute-start(f32[512,512]{1,0:T(8,128)S(1)} %constant_dynamic-update-slice_fusion.2), channel_id=1, source_target_pairs={{0,1},{1,0},{2,3},{3,2},{4,5},{5,4},{6,7},{7,6},{8,9},{9,8},{10,11... | collective-permute-start | bytes 3145736 | tf_op jit(solution)/shard_map/ppermute | solution.py:44
  402.8 3.2 collective-permute-start.18
  406.1 5.5 %collective-permute-start.19 = (f32[8,128]{1,0:T(8,128)S(1)}, f32[8,128]{1,0:T(8,128)S(1)}, u32[]{:S(2)}, u32[]{:S(2)}) collective-permute-start(f32[8,128]{1,0:T(8,128)S(1)} %broadcast_add_fusion), channel_id=1, source_target_pairs={{0,2},{1,3},{2,0},{3,1},{4,6},{5,7},{6,4},{7,5},{8,10},{9,11},{10,... | collective-permute-start | bytes 12296 | tf_op jit(solution)/shard_map/ppermute | solution.py:38
  411.5 7.0 %collective-permute-start.20 = (f32[8,128]{1,0:T(8,128)S(1)}, f32[8,128]{1,0:T(8,128)S(1)}, u32[]{:S(2)}, u32[]{:S(2)}) collective-permute-start(f32[8,128]{1,0:T(8,128)S(1)} %fusion.56), channel_id=1, source_target_pairs={{0,4},{1,5},{2,6},{3,7},{4,0},{5,1},{6,2},{7,3},{8,12},{9,13},{10,... | collective-permute-start | bytes 12296 | tf_op jit(solution)/shard_map/ppermute | solution.py:38
  418.5 5.5 %collective-permute-start.21 = (f32[8,128]{1,0:T(8,128)S(1)}, f32[8,128]{1,0:T(8,128)S(1)}, u32[]{:S(2)}, u32[]{:S(2)}) collective-permute-start(f32[8,128]{1,0:T(8,128)S(1)} %add.273), channel_id=1, source_target_pairs={{0,8},{1,9},{2,10},{3,11},{4,12},{5,13},{6,14},{7,15},{8,0},{9,1},... | collective-permute-start | bytes 12296 | tf_op jit(solution)/shard_map/ppermute | solution.py:38
  424.0 7.0 %collective-permute-start.22 = (f32[8,128]{1,0:T(8,128)S(1)}, f32[8,128]{1,0:T(8,128)S(1)}, u32[]{:S(2)}, u32[]{:S(2)}) collective-permute-start(f32[8,128]{1,0:T(8,128)S(1)} %add.274), channel_id=1, source_target_pairs={{0,16},{1,17},{2,18},{3,19},{4,20},{5,21},{6,22},{7,23},{8,24},{9,... | collective-permute-start | bytes 12296 | tf_op jit(solution)/shard_map/ppermute | solution.py:38
  431.0 5.5 %collective-permute-start.23 = (f32[8,128]{1,0:T(8,128)S(1)}, f32[8,128]{1,0:T(8,128)S(1)}, u32[]{:S(2)}, u32[]{:S(2)}) collective-permute-start(f32[8,128]{1,0:T(8,128)S(1)} %add.275), channel_id=1, source_target_pairs={{0,32},{32,0},{64,96},{96,64},{128,160},{160,128},{192,224},{224,1... | collective-permute-start | bytes 12296 | tf_op jit(solution)/shard_map/ppermute | solution.py:38
  436.5 6.4 %collective-permute-start.24 = (f32[8,128]{1,0:T(8,128)S(1)}, f32[8,128]{1,0:T(8,128)S(1)}, u32[]{:S(2)}, u32[]{:S(2)}) collective-permute-start(f32[8,128]{1,0:T(8,128)S(1)} %add.276), channel_id=1, source_target_pairs={{0,64},{32,96},{64,0},{96,32},{128,192},{160,224},{192,128},{224,1... | collective-permute-start | bytes 12296 | tf_op jit(solution)/shard_map/ppermute | solution.py:38
  442.9 9.4 %collective-permute-start.25 = (f32[8,128]{1,0:T(8,128)S(1)}, f32[8,128]{1,0:T(8,128)S(1)}, u32[]{:S(2)}, u32[]{:S(2)}) collective-permute-start(f32[8,128]{1,0:T(8,128)S(1)} %add.277), channel_id=1, source_target_pairs={{0,128},{32,160},{64,192},{96,224},{128,0},{160,32},{192,64},{224,... | collective-permute-start | bytes 12296 | tf_op jit(solution)/shard_map/ppermute | solution.py:38
  452.3 14.2 %collective-permute-start.26 = (f32[8,128]{1,0:T(8,128)S(1)}, f32[8,128]{1,0:T(8,128)S(1)}, u32[]{:S(2)}, u32[]{:S(2)}) collective-permute-start(f32[8,128]{1,0:T(8,128)S(1)} %add.278), channel_id=1, source_target_pairs={{0,256},{32,288},{64,320},{96,352},{128,384},{160,416},{192,448},{... | collective-permute-start | bytes 12296 | tf_op jit(solution)/shard_map/ppermute | solution.py:38
Sparse Core Ops, SparseCore 0:
  82.4 77.7 all-gather.2
  163.6 69.4 all-gather.4
